TPU v7x, 32 devices: a whole 2x2x4 slice. The times are simulated.
32 devices in a mesh: owner: 2 (over x), reader: 16 (over z, y, core).
Axes of the slice: x: 2, y: 2, z: 4, core: 2. Of those that a mesh axis runs over, the one named last changes fastest.
Arguments:
- acts: bfloat16 [256, 4096], P('reader', 'owner'), may hold values from -6 to 6
- grads: bfloat16 [256, 14336], P('reader', 'owner'), may hold values from -6 to 6
- basis_a: bfloat16 [4096, 4096], P('reader', 'owner'), may hold values from -0.09375 to 0.09375
- basis_g: bfloat16 [14336, 14336], P('reader', 'owner'), may hold values from -0.046875 to 0.046875
- eigvals: bfloat16 [14336, 4096], P('reader', 'owner'), may hold values from 0.099609375 to 10
- lengths: int32 [2], replicated, may hold values from 1 to 128, as said below
- shuffle: int32 [2], replicated, may hold values from 0 to 1, each once
Outputs:
- token_score: float32 [256], P('owner')
- example_score: float32 [2], replicated
Inputs may be any that keep to these rules, and one draw needn't show every extreme that they name: `lengths`: some slot has exactly 128 live tokens. `shuffle`: each example id appears once.
All inputs are finite; a program needn't handle non-finite values.
Results may differ from a plain program's by a relative error of at most 0.0003.
Values may be sent and summed in bfloat16 or wider, within the bound.
No kernel may reach another device: no remote copies, remote signals or barrier semaphores. Data moves between devices by JAX's collectives and lax.ppermute only.
A program may use at most 128 MiB of HBM per device.

v0:
```python
import jax
import jax.numpy as jnp
from jax import lax
from jax.sharding import PartitionSpec as P

D = 4096
FF = 14336
SEQ = 128


def local(acts, grads, basis_a, basis_g, eigvals, lengths, shuffle):
    owner_index = lax.axis_index("owner")
    own_length = lax.dynamic_index_in_dim(lengths, owner_index, 0, keepdims=False)
    positions = jnp.arange(SEQ, dtype=jnp.int32)
    live = (positions < own_length).astype(jnp.float32)
    partial_g = jnp.einsum(
        "tk,jk->tj",
        lax.all_gather(grads, "reader", axis=0, tiled=True),
        basis_g,
        preferred_element_type=jnp.float32,
    )
    own_g = lax.psum_scatter(partial_g, "owner", scatter_dimension=0, tiled=True)
    rot_g = (own_g * live[:, None]).astype(jnp.bfloat16)
    all_rows = lax.all_gather(acts, "reader", axis=0, tiled=True)
    own_rows = lax.all_to_all(all_rows, "owner", split_axis=0, concat_axis=1, tiled=True)
    vectors = lax.all_gather(basis_a, "owner", axis=1, tiled=True)
    own_a = jnp.einsum("tk,jk->tj", own_rows, vectors, preferred_element_type=jnp.float32)
    rot_a = (own_a * live[:, None]).astype(jnp.bfloat16)
    full_a = lax.all_gather(rot_a, "reader", axis=1, tiled=True)
    eigen_block = lax.all_gather(eigvals, "owner", axis=1, tiled=True)
    outer = jnp.einsum("tm,tn->mn", rot_g, full_a, preferred_element_type=jnp.float32)
    scaled = (outer / eigen_block.astype(jnp.float32)).astype(jnp.bfloat16)
    projected = jnp.dot(rot_g, scaled, preferred_element_type=jnp.float32)
    partial_score = jnp.sum(projected * full_a.astype(jnp.float32), axis=1) / (FF * D)
    token_score = lax.psum(partial_score, "reader")
    slot_mean = jnp.sum(token_score, keepdims=True) / SEQ
    all_means = lax.all_gather(slot_mean, "owner", axis=0, tiled=True)
    count = shuffle.shape[0]
    table = (shuffle[:, None] == jnp.arange(count, dtype=jnp.int32)[None, :]).astype(jnp.float32)
    example_score = jnp.sum(all_means[:, None] * table, axis=0)
    return (token_score, example_score)


def solution(mesh):
    return jax.shard_map(
        local,
        mesh=mesh,
        in_specs=(
            P("reader", "owner"),
            P("reader", "owner"),
            P("reader", "owner"),
            P("reader", "owner"),
            P("reader", "owner"),
            P(),
            P(),
        ),
        out_specs=(P("owner"), P()),
        check_vma=False,
    )
```

profile of v0, /device:TPU:0, one launch (start us, length us, event | category | flops | bytes accessed | tf_op | source)
XLA Modules:
  0.0 346.0 jit_solution(8944493307228276584)
XLA Ops:
  7.2 0.0 all-gather.8.cloned.1.call-start
  7.2 0.7 all-gather.8.cloned.1.call-update
  7.9 0.0 all-gather.10.cloned.1.call-start
  7.9 0.7 all-gather.10.cloned.1.call-update
  8.6 0.0 all-gather.6.cloned.1.call-start
  8.7 0.7 all-gather.6.cloned.1.call-update
  9.4 41.5 %all-gather.8.cloned.1.call-done = bf16[256,2048]{1,0:T(8,128)(2,1)} async-done(((bf16[16,2048]{1,0:T(8,128)(2,1)}), bf16[256,2048]{1,0:T(8,128)(2,1)}) %all-gather.8.cloned.1.call-update) | async-done | bytes 1048592 | tf_op jit(solution)/shard_map/all_gather | solution.py:24
  50.8 3.6 %all-to-all-start = ((bf16[2,128,2048]{2,1,0:T(8,128)(2,1)}), bf16[2,128,2048]{2,1,0:T(8,128)(2,1)S(1)}, u32[]{:S(2)}, u32[]{:S(2)}) async-start(bf16[2,128,2048]{2,1,0:T(8,128)(2,1)} %bitcast.13), calls=%async_computation.1 | async-start | bytes 2097152 | tf_op jit(solution)/shard_map/all_to_all | solution.py:25
  54.4 0.0 all-gather.12.cloned.1.call-start
  54.5 1.2 dynamic_slice.4
  55.7 0.6 compare_convert_fusion
  56.4 19.8 %all-to-all-done = bf16[2,128,2048]{2,1,0:T(8,128)(2,1)S(1)} async-done(((bf16[2,128,2048]{2,1,0:T(8,128)(2,1)}), bf16[2,128,2048]{2,1,0:T(8,128)(2,1)S(1)}, u32[]{:S(2)}, u32[]{:S(2)}) %all-to-all-start) | async-done | bytes 1048608 | tf_op jit(solution)/shard_map/all_to_all | solution.py:25
  76.2 0.7 copy.10
  76.9 14.5 %all-gather.10.cloned.1.call-done = bf16[256,4096]{1,0:T(8,128)(2,1)} async-done(((bf16[256,2048]{1,0:T(8,128)(2,1)}), bf16[256,4096]{1,0:T(8,128)(2,1)}) %all-gather.10.cloned.1.call-update) | async-done | bytes 2097168 | tf_op jit(solution)/shard_map/all_gather | solution.py:26
  91.4 3.1 fusion.5
  94.5 0.0 all-gather.12.cloned.1.call-update
  94.5 0.0 all-gather.14.cloned.1.call-start
  94.6 0.5 all-gather.14.cloned.1.call-update
  95.1 0.0 copy-start.1
  95.1 0.0 reduce-scatter.2.cloned.1.call-start
  95.2 44.1 %all-gather.6.cloned.1.call-done = bf16[256,7168]{1,0:T(8,128)(2,1)} async-done(((bf16[16,7168]{1,0:T(8,128)(2,1)}), bf16[256,7168]{1,0:T(8,128)(2,1)}) %all-gather.6.cloned.1.call-update) | async-done | bytes 3670032 | tf_op jit(solution)/shard_map/all_gather | solution.py:18
  139.3 10.7 %fusion.9 = f32[256,896]{1,0:T(8,128)} fusion(bf16[256,7168]{1,0:T(8,128)(2,1)} %all-gather.6.cloned.1.call-done, bf16[896,7168]{1,0:T(8,128)(2,1)} %param.10), kind=kOutput, calls=%fused_computation.13 | convolution fusion | flops 3288334336 | bytes 17432576 | tf_op jit(solution)/shard_map/tk,jk->tj/dot_general | solution.py:16
  149.9 0.0 reduce-scatter.2.cloned.1.call-update
  150.0 0.0 copy-done.1
  150.0 0.6 dynamic-slice
  150.5 0.0 copy-start
  150.5 26.6 %all-gather.12.cloned.1.call-done = bf16[128,4096]{1,0:T(8,128)(2,1)} async-done(((bf16[128,256]{1,0:T(8,128)(2,1)}), bf16[128,4096]{1,0:T(8,128)(2,1)}) %all-gather.12.cloned.1.call-update) | async-done | bytes 1048592 | tf_op jit(solution)/shard_map/all_gather | solution.py:29
  177.1 93.1 %all-gather.14.cloned.1.call-done = bf16[896,4096]{1,0:T(8,128)(2,1)} async-done(((bf16[896,2048]{1,0:T(8,128)(2,1)}), bf16[896,4096]{1,0:T(8,128)(2,1)}) %all-gather.14.cloned.1.call-update) | async-done | bytes 7340048 | tf_op jit(solution)/shard_map/all_gather | solution.py:30
  270.3 21.0 %reduce-scatter.2.cloned.1.call-done = f32[128,896]{1,0:T(8,128)} async-done(((f32[256,896]{1,0:T(8,128)}), f32[128,896]{1,0:T(8,128)}) %reduce-scatter.2.cloned.1.call-update) | async-done | bytes 458768 | tf_op jit(solution)/shard_map/reduce_scatter | solution.py:22
  291.3 7.3 %fusion.4 = f32[128]{0:T(128)S(1)} fusion(bf16[128,4096]{1,0:T(8,128)(2,1)} %all-gather.12.cloned.1.call-done, bf16[896,4096]{1,0:T(8,128)(2,1)} %all-gather.14.cloned.1.call-done, f32[128,896]{1,0:T(8,128)} %reduce-scatter.2.cloned.1.call-done, f32[128]{0:T(128)S(1)} %compare_convert_fusion), kind=kOutput, calls=%fused_computation.4 | convolution fusion | flops 1892089728 | bytes 8848384 | tf_op jit(solution)/shard_map/dot_general | solution.py:33
  298.6 33.2 %psum.7 = f32[128]{0:T(128)S(1)} all-reduce(f32[128]{0:T(128)S(1)} %broadcast_multiply_fusion), channel_id=1, replica_groups=mesh['owner'=2,'reader'=16] {'reader'}, use_global_device_ids=true, to_apply=%region_2.3 | all-reduce | flops 128 | bytes 1024 | tf_op jit(solution)/shard_map/psum | solution.py:35
  331.7 0.0 copy-start.2
  331.7 0.6 reduce_sum.28
  333.0 0.7 dynamic-update-slice
  333.7 4.9 %all-reduce = f32[2]{0:T(128)S(1)} all-reduce(f32[2]{0:T(128)S(1)} %dynamic-update-slice), channel_id=1, replica_groups=mesh['owner'=2,'reader'=16] {'owner'}, use_global_device_ids=true, to_apply=%add | all-reduce | flops 2 | bytes 16
  338.6 0.0 copy-done
  338.6 0.6 fusion.8
  339.2 0.0 copy-done.2
  (2 shorter events, 0.0 us)
Async XLA Ops:
  7.2 43.7 %all-gather.8.cloned.1.call-start = ((), (), s32[]{:S(2)}) async-start(), calls=%async_computation.4 | async-start | bytes 1114112 | tf_op jit(solution)/shard_map/all_gather | solution.py:24
  7.9 83.5 %all-gather.10.cloned.1.call-start = ((), (), s32[]{:S(2)}) async-start(), calls=%async_computation.5 | async-start | bytes 3145728 | tf_op jit(solution)/shard_map/all_gather | solution.py:26
  8.6 130.6 %all-gather.6.cloned.1.call-start = ((), (), s32[]{:S(2)}) async-start(), calls=%async_computation.2 | async-start | bytes 3899392 | tf_op jit(solution)/shard_map/all_gather | solution.py:18
  50.8 25.4 %all-to-all-start = ((bf16[2,128,2048]{2,1,0:T(8,128)(2,1)}), bf16[2,128,2048]{2,1,0:T(8,128)(2,1)S(1)}, u32[]{:S(2)}, u32[]{:S(2)}) async-start(bf16[2,128,2048]{2,1,0:T(8,128)(2,1)} %bitcast.13), calls=%async_computation.1 | async-start | bytes 2097152 | tf_op jit(solution)/shard_map/all_to_all | solution.py:25
  54.4 122.7 %all-gather.12.cloned.1.call-start = ((), (), s32[]{:S(2)}) async-start(), calls=%async_computation.6 | async-start | bytes 1114112 | tf_op jit(solution)/shard_map/all_gather | solution.py:29
  94.5 175.7 %all-gather.14.cloned.1.call-start = ((), (), s32[]{:S(2)}) async-start(), calls=%async_computation.7 | async-start | bytes 11010048 | tf_op jit(solution)/shard_map/all_gather | solution.py:30
  95.1 54.9 %copy-start.1 = (u32[32]{0:T(128)S(1)}, u32[32]{0:T(128)}, u32[]{:S(2)}) copy-start(u32[32]{0:T(128)} %constant.24) | copy-start | bytes 388
  95.1 196.1 %reduce-scatter.2.cloned.1.call-start = ((), (), s32[]{:S(2)}) async-start(), calls=%async_computation.3 | async-start | bytes 1376256 | tf_op jit(solution)/shard_map/reduce_scatter | solution.py:22
  150.5 188.0 %copy-start = (s32[2]{0:T(128)S(1)}, s32[2]{0:T(128)}, u32[]{:S(2)}) copy-start(s32[2]{0:T(128)} %param.13) | copy-start | bytes 28
  331.7 7.4 %copy-start.2 = (f32[128]{0:T(128)}, f32[128]{0:T(128)S(1)}, u32[]{:S(2)}) copy-start(f32[128]{0:T(128)S(1)} %psum.7) | copy-start | bytes 1540
Sparse Core Ops, SparseCore 0:
  10.2 40.6 all-gather.7
  52.4 39.0 all-gather.9
  93.7 45.4 all-gather.5
  141.3 35.8 all-gather.11
  178.5 91.6 all-gather.13
  272.4 18.8 reduce-scatter.1
where the time goes:
time: 346 us
  waiting for transfers between devices  263 us (76%)
  blocking collectives  38.1 us (11%)
  matrix products  21.1 us (6%)
  between operations  14.8 us (4%)
  starting transfers between devices  3.81 us (1%)
    all_gather x1, waiting for transfers between devices, local(): eigen_block = lax.all_gather(eigvals, 'owner', axis=1, tiled=True)  93.1 us
    all_gather x1, waiting for transfers between devices, local(): lax.all_gather(grads, 'reader', axis=0, tiled=True)  44.1 us
    all_gather x1, waiting for transfers between devices, local(): all_rows = lax.all_gather(acts, 'reader', axis=0, tiled=True)  41.5 us
    psum x1, blocking collectives, local(): token_score = lax.psum(partial_score, 'reader')  33.2 us
    all_gather x1, waiting for transfers between devices, local(): full_a = lax.all_gather(rot_a, 'reader', axis=1, tiled=True)  26.6 us
    reduce_scatter x1, waiting for transfers between devices, local(): lax.psum_scatter(partial_g, 'owner', scatter_dimension=0, tiled=True)  21 us
    all_to_all x1, waiting for transfers between devices, local(): lax.all_to_all(all_rows, 'owner', split_axis=0, concat_axis=1, tiled=True)  19.8 us
    all_gather x1, waiting for transfers between devices, local(): vectors = lax.all_gather(basis_a, 'owner', axis=1, tiled=True)  14.5 us
  transfers between devices with their start and end apart: 7, of which 7 were waited for; matrix products, arithmetic and copies ran while one was open for 5% of the time, Pallas kernels for 0%

commit v1 on v0

--- a/solution.py
+++ b/solution.py
@@ -2,6 +2,7 @@
 import jax.numpy as jnp
 from jax import lax
 from jax.sharding import PartitionSpec as P
+from jax.lax import all_to_all, axis_size
 
 D = 4096
 FF = 14336
@@ -22,7 +23,11 @@
     own_g = lax.psum_scatter(partial_g, "owner", scatter_dimension=0, tiled=True)
     rot_g = (own_g * live[:, None]).astype(jnp.bfloat16)
     all_rows = lax.all_gather(acts, "reader", axis=0, tiled=True)
-    own_rows = lax.all_to_all(all_rows, "owner", split_axis=0, concat_axis=1, tiled=True)
+    reply = axis_size("owner")
+    high = jnp.split(all_rows, reply, axis=0)
+    long_array = jnp.stack(high)
+    all_values = all_to_all(long_array, axis_name="owner", split_axis=0, concat_axis=0)
+    own_rows = jnp.concatenate(all_values, axis=1)
     vectors = lax.all_gather(basis_a, "owner", axis=1, tiled=True)
     own_a = jnp.einsum("tk,jk->tj", own_rows, vectors, preferred_element_type=jnp.float32)
     rot_a = (own_a * live[:, None]).astype(jnp.bfloat16)

time: 346 us -> 349 us (level)
    all_gather x1, waiting for transfers between devices: 14.5 us -> 35.7 us  [local(): vectors = lax.all_gather(basis_a, 'owner', axis=1, tiled=True)]
    all_to_all x1, waiting for transfers between devices: 19.8 us -> 0.01 us  [local(): all_to_all(long_array, axis_name='owner', split_axis=0, concat_axis=0)]
  transfers between devices with their start and end apart: 7 -> 7, of which waited for: 7 -> 6; matrix products, arithmetic and copies ran while one was open for 5% -> 5% of each run, Pallas kernels for 0% -> 0%
where the time goes in v1:
time: 349 us
  waiting for transfers between devices  264 us (76%)
  blocking collectives  38.1 us (11%)
  matrix products  21 us (6%)
  between operations  14.9 us (4%)
  local copies, waits for them, and re-layouts  3.86 us (1%)
  starting transfers between devices  3.81 us (1%)
    all_gather x1, waiting for transfers between devices, local(): eigen_block = lax.all_gather(eigvals, 'owner', axis=1, tiled=True)  93.1 us
    all_gather x1, waiting for transfers between devices, local(): lax.all_gather(grads, 'reader', axis=0, tiled=True)  44.1 us
    all_gather x1, waiting for transfers between devices, local(): all_rows = lax.all_gather(acts, 'reader', axis=0, tiled=True)  41.5 us
    all_gather x1, waiting for transfers between devices, local(): vectors = lax.all_gather(basis_a, 'owner', axis=1, tiled=True)  35.7 us
    psum x1, blocking collectives, local(): token_score = lax.psum(partial_score, 'reader')  33.2 us
    all_gather x1, waiting for transfers between devices, local(): full_a = lax.all_gather(rot_a, 'reader', axis=1, tiled=True)  26.5 us
    reduce_scatter x1, waiting for transfers between devices, local(): lax.psum_scatter(partial_g, 'owner', scatter_dimension=0, tiled=True)  21 us
    dot_general x1, matrix products, local(): jnp.einsum('tk,jk->tj', lax.all_gather(grads, 'reader', axis=0, tiled=Tru...  10.7 us
  transfers between devices with their start and end apart: 7, of which 6 were waited for; matrix products, arithmetic and copies ran while one was open for 5% of the time, Pallas kernels for 0%

profile of v1, /device:TPU:0, one launch (start us, length us, event | category | flops | bytes accessed | tf_op | source)
XLA Modules:
  0.0 349.1 jit_solution(17200239072719104446)
XLA Ops:
  7.2 0.0 copy-start
  7.2 0.0 all-gather.8.cloned.1.call-start
  7.2 0.7 all-gather.8.cloned.1.call-update
  7.9 0.0 all-gather.10.cloned.1.call-start
  8.0 0.7 all-gather.10.cloned.1.call-update
  8.7 0.0 all-gather.6.cloned.1.call-start
  8.7 0.7 all-gather.6.cloned.1.call-update
  9.4 41.5 %all-gather.8.cloned.1.call-done = bf16[256,2048]{1,0:T(8,128)(2,1)} async-done(((bf16[16,2048]{1,0:T(8,128)(2,1)}), bf16[256,2048]{1,0:T(8,128)(2,1)}) %all-gather.8.cloned.1.call-update) | async-done | bytes 1048592 | tf_op jit(solution)/shard_map/all_gather | solution.py:25
  50.8 1.3 fusion.9
  52.1 0.3 copy.14
  52.4 0.3 copy.15
  52.7 1.1 pad_maximum_fusion
  53.8 3.6 %all-to-all-start = ((bf16[2,128,2048]{1,2,0:T(8,128)(2,1)}), bf16[2,128,2048]{1,2,0:T(8,128)(2,1)S(1)}, u32[]{:S(2)}, u32[]{:S(2)}) async-start(bf16[2,128,2048]{1,2,0:T(8,128)(2,1)} %pad_maximum_fusion), calls=%async_computation.1 | async-start | bytes 2097152 | tf_op jit(solution)/shard_map/all_to_all | solution.py:29
  57.3 0.0 all-gather.12.cloned.1.call-start
  57.4 0.0 copy-done
  57.4 0.6 dynamic_slice.4
  58.0 0.7 compare_convert_fusion
  58.7 35.7 %all-gather.10.cloned.1.call-done = bf16[256,4096]{1,0:T(8,128)(2,1)} async-done(((bf16[256,2048]{1,0:T(8,128)(2,1)}), bf16[256,4096]{1,0:T(8,128)(2,1)}) %all-gather.10.cloned.1.call-update) | async-done | bytes 2097168 | tf_op jit(solution)/shard_map/all_gather | solution.py:31
  94.3 0.0 all-to-all-done
  94.3 3.1 fusion.5
  97.4 0.0 all-gather.12.cloned.1.call-update
  97.4 0.0 all-gather.14.cloned.1.call-start
  97.5 0.5 all-gather.14.cloned.1.call-update
  98.0 0.0 copy-start.2
  98.0 0.0 reduce-scatter.2.cloned.1.call-start
  98.1 44.1 %all-gather.6.cloned.1.call-done = bf16[256,7168]{1,0:T(8,128)(2,1)} async-done(((bf16[16,7168]{1,0:T(8,128)(2,1)}), bf16[256,7168]{1,0:T(8,128)(2,1)}) %all-gather.6.cloned.1.call-update) | async-done | bytes 3670032 | tf_op jit(solution)/shard_map/all_gather | solution.py:19
  142.2 10.7 %fusion.10 = f32[256,896]{1,0:T(8,128)} fusion(bf16[256,7168]{1,0:T(8,128)(2,1)} %all-gather.6.cloned.1.call-done, bf16[896,7168]{1,0:T(8,128)(2,1)} %param.10), kind=kOutput, calls=%fused_computation.15 | convolution fusion | flops 3288334336 | bytes 17432576 | tf_op jit(solution)/shard_map/tk,jk->tj/dot_general | solution.py:17
  152.9 0.0 reduce-scatter.2.cloned.1.call-update
  152.9 0.0 copy-done.2
  152.9 0.7 dynamic-slice
  153.6 0.0 copy-start.1
  153.6 26.5 %all-gather.12.cloned.1.call-done = bf16[128,4096]{1,0:T(8,128)(2,1)} async-done(((bf16[128,256]{1,0:T(8,128)(2,1)}), bf16[128,4096]{1,0:T(8,128)(2,1)}) %all-gather.12.cloned.1.call-update) | async-done | bytes 1048592 | tf_op jit(solution)/shard_map/all_gather | solution.py:34
  180.1 93.1 %all-gather.14.cloned.1.call-done = bf16[896,4096]{1,0:T(8,128)(2,1)} async-done(((bf16[896,2048]{1,0:T(8,128)(2,1)}), bf16[896,4096]{1,0:T(8,128)(2,1)}) %all-gather.14.cloned.1.call-update) | async-done | bytes 7340048 | tf_op jit(solution)/shard_map/all_gather | solution.py:35
  273.2 21.0 %reduce-scatter.2.cloned.1.call-done = f32[128,896]{1,0:T(8,128)} async-done(((f32[256,896]{1,0:T(8,128)}), f32[128,896]{1,0:T(8,128)}) %reduce-scatter.2.cloned.1.call-update) | async-done | bytes 458768 | tf_op jit(solution)/shard_map/reduce_scatter | solution.py:23
  294.2 7.3 %fusion.4 = f32[128]{0:T(128)S(1)} fusion(bf16[128,4096]{1,0:T(8,128)(2,1)} %all-gather.12.cloned.1.call-done, bf16[896,4096]{1,0:T(8,128)(2,1)} %all-gather.14.cloned.1.call-done, f32[128,896]{1,0:T(8,128)} %reduce-scatter.2.cloned.1.call-done, f32[128]{0:T(128)S(1)} %compare_convert_fusion), kind=kOutput, calls=%fused_computation.4 | convolution fusion | flops 1892089728 | bytes 8848384 | tf_op jit(solution)/shard_map/dot_general | solution.py:38
  301.5 33.2 %psum.7 = f32[128]{0:T(128)S(1)} all-reduce(f32[128]{0:T(128)S(1)} %broadcast_multiply_fusion), channel_id=1, replica_groups=mesh['owner'=2,'reader'=16] {'reader'}, use_global_device_ids=true, to_apply=%region_2.3 | all-reduce | flops 128 | bytes 1024 | tf_op jit(solution)/shard_map/psum | solution.py:40
  334.6 0.0 copy-start.3
  334.6 0.6 reduce_sum.28
  335.9 0.8 dynamic-update-slice
  336.7 4.9 %all-reduce = f32[2]{0:T(128)S(1)} all-reduce(f32[2]{0:T(128)S(1)} %dynamic-update-slice), channel_id=1, replica_groups=mesh['owner'=2,'reader'=16] {'owner'}, use_global_device_ids=true, to_apply=%add | all-reduce | flops 2 | bytes 16
  341.6 0.0 copy-done.1
  341.6 0.6 fusion.8
  342.2 0.0 copy-done.3
  (2 shorter events, 0.0 us)
Async XLA Ops:
  7.2 50.2 %copy-start = (s32[2]{0:T(128)S(1)}, s32[2]{0:T(128)}, u32[]{:S(2)}) copy-start(s32[2]{0:T(128)} %param.12) | copy-start | bytes 28
  7.2 43.7 %all-gather.8.cloned.1.call-start = ((), (), s32[]{:S(2)}) async-start(), calls=%async_computation.4 | async-start | bytes 1114112 | tf_op jit(solution)/shard_map/all_gather | solution.py:25
  7.9 86.4 %all-gather.10.cloned.1.call-start = ((), (), s32[]{:S(2)}) async-start(), calls=%async_computation.5 | async-start | bytes 3145728 | tf_op jit(solution)/shard_map/all_gather | solution.py:31
  8.7 133.5 %all-gather.6.cloned.1.call-start = ((), (), s32[]{:S(2)}) async-start(), calls=%async_computation.2 | async-start | bytes 3899392 | tf_op jit(solution)/shard_map/all_gather | solution.py:19
  53.8 40.6 %all-to-all-start = ((bf16[2,128,2048]{1,2,0:T(8,128)(2,1)}), bf16[2,128,2048]{1,2,0:T(8,128)(2,1)S(1)}, u32[]{:S(2)}, u32[]{:S(2)}) async-start(bf16[2,128,2048]{1,2,0:T(8,128)(2,1)} %pad_maximum_fusion), calls=%async_computation.1 | async-start | bytes 2097152 | tf_op jit(solution)/shard_map/all_to_all | solution.py:29
  57.3 122.7 %all-gather.12.cloned.1.call-start = ((), (), s32[]{:S(2)}) async-start(), calls=%async_computation.6 | async-start | bytes 1114112 | tf_op jit(solution)/shard_map/all_gather | solution.py:34
  97.4 175.7 %all-gather.14.cloned.1.call-start = ((), (), s32[]{:S(2)}) async-start(), calls=%async_computation.7 | async-start | bytes 11010048 | tf_op jit(solution)/shard_map/all_gather | solution.py:35
  98.0 54.9 %copy-start.2 = (u32[32]{0:T(128)S(1)}, u32[32]{0:T(128)}, u32[]{:S(2)}) copy-start(u32[32]{0:T(128)} %constant.24) | copy-start | bytes 388
  98.0 196.1 %reduce-scatter.2.cloned.1.call-start = ((), (), s32[]{:S(2)}) async-start(), calls=%async_computation.3 | async-start | bytes 1376256 | tf_op jit(solution)/shard_map/reduce_scatter | solution.py:23
  153.6 188.1 %copy-start.1 = (s32[2]{0:T(128)S(1)}, s32[2]{0:T(128)}, u32[]{:S(2)}) copy-start(s32[2]{0:T(128)} %param.13) | copy-start | bytes 28
  334.6 7.6 %copy-start.3 = (f32[128]{0:T(128)}, f32[128]{0:T(128)S(1)}, u32[]{:S(2)}) copy-start(f32[128]{0:T(128)S(1)} %psum.7) | copy-start | bytes 1540
Sparse Core Ops, SparseCore 0:
  10.2 40.6 all-gather.7
  52.4 41.9 all-gather.9
  96.6 45.4 all-gather.5
  144.2 35.8 all-gather.11
  181.5 91.6 all-gather.13
  275.3 18.8 reduce-scatter.1
